TPU v7x, 32 devices: a whole 2x2x4 slice. The times are simulated.
32 devices in a mesh: lines: 2 (over x), col: 16 (over z, y, core).
Axes of the slice: x: 2, y: 2, z: 4, core: 2. Of those that a mesh axis runs over, the one named last changes fastest.
Arguments:
- primary: float32 [16, 4, 128, 256], P(None, 'lines', 'col'), parts along dimension 1, may hold values from -6 to 6
- conductivity: float32 [128, 512], P('col', 'lines'), parts along dimension 1, may hold values from 0.1 to 10
- wavenumbers: float32 [16], replicated, may hold values from 0.05 to 1.5
- quadrature: float32 [16], replicated, may hold values from 0.02 to 0.2
- electrodes: int32 [64], P(('lines', 'col')), parts along dimension 0, may hold values from 0 to 127, as said below
- far_pole: int32 [4, 32], P('lines'), parts along dimension 0, may hold values from 0 to 31, as said below
- observed: float32 [4, 32], P('lines'), parts along dimension 0, may hold values from -6 to 6
- prior_adjoint: float32 [16, 4, 128, 256], P(None, 'lines', 'col'), parts along dimension 1, may hold values from -0.012 to 0.012
Outputs:
- predicted: float32 [4, 32], P('lines'), parts along dimension 0
- gradient: float32 [128, 512], P('col', 'lines'), parts along dimension 1
There are 2 independent parts, one for each index of `lines`. A program takes and returns all parts, laid end to end along the dimension named above; an argument that names none is the same for every part. Nothing has to cross between parts.
Inputs may be any that keep to these rules, and one draw needn't show every extreme that they name: electrodes[e] lies in columns 4 e to 4 e + 3. far_pole[s, r] differs from r by 1 to 8.
All inputs are finite; a program needn't handle non-finite values.
Results may differ from a plain program's by a relative error of at most 0.0003.
Values sent between devices are 32-bit elements; how exact they have to be, the bound alone decides.
No kernel may reach another device: no remote copies, remote signals or barrier semaphores. Data moves between devices by JAX's collectives and lax.ppermute only.
A program may use at most 64 MiB of HBM per device.

v0:
```python
import jax
import jax.numpy as jnp
from jax import lax
from jax.sharding import PartitionSpec as P

ITERS = 2


def padded_2(block, sides, width):
    for axis, dim in sides:
        count = lax.axis_size(axis)
        forward = [(i, i + 1) for i in range(count - 1)]
        backward = [(target, source) for source, target in forward]
        low = lax.ppermute(
            lax.slice_in_dim(block, block.shape[dim] - width, None, axis=dim), axis, forward
        )
        high = lax.ppermute(lax.slice_in_dim(block, 0, width, axis=dim), axis, backward)
        block = jnp.concatenate([low, block, high], axis=dim)
    return block


def shifted(value, axis, steps):
    count = lax.axis_size(axis)
    initial, last = (max(0, -steps), min(count, count - steps))
    return lax.ppermute(value, axis, [(source, source + steps) for source in range(initial, last)])


def coefficients(sigma_wide):
    center = sigma_wide[1:-1]
    west_face = 0.5 * (center + sigma_wide[:-2])
    east_face = 0.5 * (center + sigma_wide[2:])
    below_sigma = jnp.concatenate([center[:, 1:], jnp.zeros_like(center[:, :1])], axis=1)
    lower_face = 0.5 * (center + below_sigma)
    above_sigma = jnp.concatenate([jnp.zeros_like(center[:, :1]), center[:, :-1]], axis=1)
    upper_face = 0.5 * (center + above_sigma)
    top_row = jnp.arange(center.shape[1]) == 0
    upper_face = jnp.where(top_row[None, :], 0.0, upper_face)
    return (west_face, east_face, lower_face, upper_face, center)


def stencil(field_wide, faces_set, mass_scale):
    west_face, east_face, lower_face, upper_face, center = faces_set
    middle = field_wide[..., 1:-1, :]
    below_cells = jnp.concatenate([middle[..., 1:], jnp.zeros_like(middle[..., :1])], axis=-1)
    above_cells = jnp.concatenate([jnp.zeros_like(middle[..., :1]), middle[..., :-1]], axis=-1)
    result = west_face * (middle - field_wide[..., :-2, :]) + east_face * (
        middle - field_wide[..., 2:, :]
    )
    result = result + lower_face * (middle - below_cells) + upper_face * (middle - above_cells)
    return result + mass_scale * center * middle


def local_sum(left_field, right_field):
    return jnp.sum(left_field * right_field, axis=(2, 3))


def squares(residual):
    return lax.psum(local_sum(residual, residual), "col")


def expand(scalars):
    return scalars[:, :, None, None]


def conjugate(source, first_image, operate, start):
    solution = start
    residual = source
    direction = source
    norm_now = squares(residual)
    applied = first_image
    for iteration in range(ITERS):
        if iteration > 0:
            applied = operate(direction)
        step_size = norm_now / lax.psum(local_sum(direction, applied), "col")
        solution = solution + expand(step_size) * direction
        if iteration + 1 < ITERS:
            residual = residual - expand(step_size) * applied
            norm_next = squares(residual)
            direction = residual + expand(norm_next / norm_now) * direction
            norm_now = norm_next
    return solution


def on_device(
    primary, conductivity, wavenumbers, quadrature, electrodes, far_pole, observed, prior_adjoint
):
    columns = conductivity.shape[0]
    depth_cells = conductivity.shape[1]
    device = lax.axis_index("col")
    device_count = lax.axis_size("col")
    offset = device * columns
    wide_sigma = padded_2(conductivity, (("col", 0),), 2)
    positions = offset - 2 + jnp.arange(columns + 4)
    inside = (positions >= 0) & (positions < columns * device_count)
    contrast_wide = jnp.where(inside[:, None], wide_sigma - 1.0, 0.0)
    mass_scale = (wavenumbers * wavenumbers)[:, None, None, None]
    operator_faces = coefficients(wide_sigma[1:-1])

    def operate(state):
        padded = padded_2(state, (("col", 2),), 1)
        return stencil(padded, operator_faces, mass_scale)

    padded_primary = padded_2(primary, (("col", 2),), 1)
    source = -stencil(padded_primary, coefficients(contrast_wide[1:-1]), mass_scale)
    first_image = operate(source)
    secondary = conjugate(source, first_image, operate, jnp.zeros_like(source))
    total_field = primary + secondary
    surface = total_field[:, :, :, 0]
    weighted = jnp.einsum("k,ksc->sc", quadrature, surface, precision=lax.Precision.HIGHEST)
    pick_table = (electrodes[:, None] - offset == jnp.arange(columns)[None, :]).astype(jnp.float32)
    own_potentials = jnp.einsum("sc,ec->se", weighted, pick_table, precision=lax.Precision.HIGHEST)
    potentials = lax.all_gather(own_potentials, "col", axis=1, tiled=True)
    predicted = potentials - jnp.take_along_axis(potentials, far_pole, axis=1)
    misfit = predicted - observed
    own_count = electrodes.shape[0]
    own_ids = device * own_count + jnp.arange(own_count)
    own_misfit = lax.dynamic_slice_in_dim(misfit, device * own_count, own_count, 1)
    far_hits = (far_pole[:, :, None] == own_ids[None, None, :]).astype(jnp.float32)
    returned = jnp.einsum("sr,sre->se", misfit, far_hits, precision=lax.Precision.HIGHEST)
    charge = own_misfit - returned
    charge_cols = jnp.einsum("se,ec->sc", charge, pick_table, precision=lax.Precision.HIGHEST)
    surface_row = (jnp.arange(depth_cells) == 0).astype(jnp.float32)
    adjoint_source = quadrature[:, None, None, None] * charge_cols[None, :, :, None] * surface_row
    adjoint_residual = adjoint_source - operate(prior_adjoint)
    adjoint = conjugate(adjoint_residual, operate(adjoint_residual), operate, prior_adjoint)
    edge_columns = shifted((adjoint[:, :, :1], total_field[:, :, :1]), "col", -1)
    adjoint_next = jnp.concatenate([adjoint[:, :, 1:], edge_columns[0]], axis=2)
    total_next = jnp.concatenate([total_field[:, :, 1:], edge_columns[1]], axis=2)
    adjoint_down = jnp.concatenate([adjoint[..., 1:], jnp.zeros_like(adjoint[..., :1])], axis=-1)
    total_down = jnp.concatenate(
        [total_field[..., 1:], jnp.zeros_like(total_field[..., :1])], axis=-1
    )
    correlation = (adjoint_next - adjoint) * (total_next - total_field)
    correlation = correlation + (adjoint_down - adjoint) * (total_down - total_field)
    correlation = correlation + mass_scale * adjoint * total_field
    gradient = jnp.sum(correlation, axis=(0, 1))
    return (predicted, gradient)


def solution(mesh):
    placed = (
        P(None, "lines", "col", None),
        P("col", "lines"),
        P(),
        P(),
        P(("lines", "col")),
        P("lines", None),
        P("lines", None),
        P(None, "lines", "col", None),
    )
    return jax.shard_map(
        on_device,
        mesh=mesh,
        in_specs=placed,
        out_specs=(P("lines", None), P("col", "lines")),
        check_vma=False,
    )
```

profile of v0, /device:TPU:1, one launch (start us, length us, event | category | flops | bytes accessed | tf_op | source)
XLA Modules:
  0.0 319.6 jit_solution(12586996976462141782)
XLA Ops:
  0.6 0.8 fusion.97
  1.4 1.9 collective-permute-start.1
  3.3 4.5 %collective-permute-start = (f32[2,256]{1,0:T(2,128)S(1)}, f32[2,256]{1,0:T(2,128)S(1)}, u32[]{:S(2)}, u32[]{:S(2)}) collective-permute-start(f32[2,256]{1,0:T(2,128)S(1)} %get-tuple-element.61), channel_id=1, source_target_pairs={{0,1},{1,2},{2,3},{3,4},{4,5},{5,6},{6,7},{7,8},{8,9},{9,10},{10,1... | collective-permute-start | bytes 6152 | tf_op jit(solution)/shard_map/ppermute | solution.py:14
  7.9 1.1 fusion.93
  9.0 1.9 collective-permute-start.3
  10.9 3.6 %collective-permute-start.2 = (f32[16,2,1,256]{3,2,1,0:T(1,128)S(1)}, f32[16,2,1,256]{3,2,1,0:T(1,128)S(1)}, u32[]{:S(2)}, u32[]{:S(2)}) collective-permute-start(f32[16,2,1,256]{3,2,1,0:T(1,128)S(1)} %get-tuple-element.44), channel_id=1, source_target_pairs={{0,1},{1,2},{2,3},{3,4},{4,5},{5,6},{6,7},{7,8},{8,9},{9,10},{10,1... | collective-permute-start | bytes 98312 | tf_op jit(solution)/shard_map/ppermute | solution.py:14
  14.5 1.1 fusion.88
  15.6 1.9 collective-permute-start.9
  20.8 3.6 %collective-permute-start.8 = (f32[16,2,1,256]{3,2,1,0:T(1,128)S(1)}, f32[16,2,1,256]{3,2,1,0:T(1,128)S(1)}, u32[]{:S(2)}, u32[]{:S(2)}) collective-permute-start(f32[16,2,1,256]{3,2,1,0:T(1,128)S(1)} %get-tuple-element.34), channel_id=1, source_target_pairs={{0,1},{1,2},{2,3},{3,4},{4,5},{5,6},{6,7},{7,8},{8,9},{9,10},{10,1... | collective-permute-start | bytes 98312 | tf_op jit(solution)/shard_map/ppermute | solution.py:14
  25.1 1.9 collective-permute-start.5
  27.1 3.6 %collective-permute-start.4 = (f32[16,2,1,256]{3,2,1,0:T(1,128)S(1)}, f32[16,2,1,256]{3,2,1,0:T(1,128)S(1)}, u32[]{:S(2)}, u32[]{:S(2)}) collective-permute-start(f32[16,2,1,256]{3,2,1,0:T(1,128)S(1)} %get-tuple-element.40), channel_id=1, source_target_pairs={{0,1},{1,2},{2,3},{3,4},{4,5},{5,6},{6,7},{7,8},{8,9},{9,10},{10,1... | collective-permute-start | bytes 98312 | tf_op jit(solution)/shard_map/ppermute | solution.py:14
  30.9 0.9 collective-permute-done.4
  32.1 55.7 %all-reduce.19 = (f32[16,2]{1,0:T(8,128)S(1)}, f32[16,2]{1,0:T(8,128)S(1)}) all-reduce(f32[16,2]{1,0:T(8,128)S(1)} %get-tuple-element.13, f32[16,2]{1,0:T(8,128)S(1)} %get-tuple-element.12), channel_id=1, replica_groups=mesh['lines'=2,'col'=16] {'col'}, use_global_device_ids=true, to_apply=%region_1.2 | all-reduce | flops 64 | bytes 512 | tf_op jit(solution)/shard_map/psum | solution.py:58
  88.1 34.4 %psum.58 = f32[16,2]{1,0:T(8,128)S(1)} all-reduce(f32[16,2]{1,0:T(8,128)S(1)} %multiply_reduce_fusion.3), channel_id=1, replica_groups=mesh['lines'=2,'col'=16] {'col'}, use_global_device_ids=true, to_apply=%region_5.6 | all-reduce | flops 32 | bytes 256 | tf_op jit(solution)/shard_map/psum | solution.py:58
  122.7 2.5 collective-permute-start.7
  125.2 3.1 collective-permute-start.6
  128.5 0.9 collective-permute-done.6
  129.7 28.5 %psum.59 = f32[16,2]{1,0:T(8,128)S(1)} all-reduce(f32[16,2]{1,0:T(8,128)S(1)} %fusion.55), channel_id=1, replica_groups=mesh['lines'=2,'col'=16] {'col'}, use_global_device_ids=true, to_apply=%region_7.8 | all-reduce | flops 32 | bytes 256 | tf_op jit(solution)/shard_map/psum | solution.py:74
  159.4 19.0 %all-gather = f32[16,2,2]{2,1,0:T(2,128)S(1)} all-gather(f32[1,2,2]{2,1,0:T(2,128)S(1)} %convolution_bitcast_fusion), channel_id=1, replica_groups=mesh['lines'=2,'col'=16] {'col'}, dimensions={0}, use_global_device_ids=true | all-gather | bytes 272 | tf_op jit(solution)/shard_map/all_gather | solution.py:112
  178.5 0.9 gather_fusion
  181.5 2.1 collective-permute-start.11
  183.6 3.5 %collective-permute-start.10 = (f32[16,2,1,256]{3,2,1,0:T(1,128)S(1)}, f32[16,2,1,256]{3,2,1,0:T(1,128)S(1)}, u32[]{:S(2)}, u32[]{:S(2)}) collective-permute-start(f32[16,2,1,256]{3,2,1,0:T(1,128)S(1)} %get-tuple-element.28), channel_id=1, source_target_pairs={{0,1},{1,2},{2,3},{3,4},{4,5},{5,6},{6,7},{7,8},{8,9},{9,10},{10,1... | collective-permute-start | bytes 98312 | tf_op jit(solution)/shard_map/ppermute | solution.py:14
  187.2 1.9 collective-permute-start.15
  189.6 53.5 %all-reduce.18 = (f32[16,2]{1,0:T(8,128)S(1)}, f32[16,2]{1,0:T(8,128)S(1)}) all-reduce(f32[16,2]{1,0:T(8,128)S(1)} %get-tuple-element.11, f32[16,2]{1,0:T(8,128)S(1)} %get-tuple-element.10), channel_id=1, replica_groups=mesh['lines'=2,'col'=16] {'col'}, use_global_device_ids=true, to_apply=%region_9.10 | all-reduce | flops 64 | bytes 512 | tf_op jit(solution)/shard_map/psum | solution.py:58
  243.3 34.4 %psum.62 = f32[16,2]{1,0:T(8,128)S(1)} all-reduce(f32[16,2]{1,0:T(8,128)S(1)} %multiply_reduce_fusion), channel_id=1, replica_groups=mesh['lines'=2,'col'=16] {'col'}, use_global_device_ids=true, to_apply=%region_13.14 | all-reduce | flops 32 | bytes 256 | tf_op jit(solution)/shard_map/psum | solution.py:58
  277.9 2.5 collective-permute-start.13
  280.5 3.1 collective-permute-start.12
  283.7 0.9 collective-permute-done.12
  284.9 28.5 %psum.63 = f32[16,2]{1,0:T(8,128)S(1)} all-reduce(f32[16,2]{1,0:T(8,128)S(1)} %fusion.56), channel_id=1, replica_groups=mesh['lines'=2,'col'=16] {'col'}, use_global_device_ids=true, to_apply=%region_15.16 | all-reduce | flops 32 | bytes 256 | tf_op jit(solution)/shard_map/psum | solution.py:74
  313.6 3.9 %collective-permute-start.14 = (f32[16,2,1,256]{3,2,1,0:T(1,128)S(1)}, f32[16,2,1,256]{3,2,1,0:T(1,128)S(1)}, u32[]{:S(2)}, u32[]{:S(2)}) collective-permute-start(f32[16,2,1,256]{3,2,1,0:T(1,128)S(1)} %slice.266), channel_id=1, source_target_pairs={{1,0},{2,1},{3,2},{4,3},{5,4},{6,5},{7,6},{8,7},{9,8},{10,9},{11,1... | collective-permute-start | bytes 98312 | tf_op jit(solution)/shard_map/ppermute | solution.py:25
  317.8 1.0 collective-permute-done.14
  318.8 0.8 fusion.54
  (86 shorter events, 10.5 us)
Async XLA Ops:
  0.6 16.9 %copy-start = (f32[16,2,8,256]{3,2,1,0:T(8,128)S(1)}, f32[16,2,8,256]{3,2,1,0:T(8,128)}, u32[]{:S(2)}) copy-start(f32[16,2,8,256]{3,2,1,0:T(8,128)} %param.8) | copy-start | bytes 786436
  1.4 19.4 %collective-permute-start.1 = (f32[2,256]{1,0:T(2,128)S(1)}, f32[2,256]{1,0:T(2,128)S(1)}, u32[]{:S(2)}, u32[]{:S(2)}) collective-permute-start(f32[2,256]{1,0:T(2,128)S(1)} %get-tuple-element.62), channel_id=1, source_target_pairs={{1,0},{2,1},{3,2},{4,3},{5,4},{6,5},{7,6},{8,7},{9,8},{10,9},{11,1... | collective-permute-start | bytes 6152 | tf_op jit(solution)/shard_map/ppermute | solution.py:17
  3.3 21.1 %collective-permute-start = (f32[2,256]{1,0:T(2,128)S(1)}, f32[2,256]{1,0:T(2,128)S(1)}, u32[]{:S(2)}, u32[]{:S(2)}) collective-permute-start(f32[2,256]{1,0:T(2,128)S(1)} %get-tuple-element.61), channel_id=1, source_target_pairs={{0,1},{1,2},{2,3},{3,4},{4,5},{5,6},{6,7},{7,8},{8,9},{9,10},{10,1... | collective-permute-start | bytes 6152 | tf_op jit(solution)/shard_map/ppermute | solution.py:14
  9.0 15.9 %collective-permute-start.3 = (f32[16,2,1,256]{3,2,1,0:T(1,128)S(1)}, f32[16,2,1,256]{3,2,1,0:T(1,128)S(1)}, u32[]{:S(2)}, u32[]{:S(2)}) collective-permute-start(f32[16,2,1,256]{3,2,1,0:T(1,128)S(1)} %get-tuple-element.45), channel_id=1, source_target_pairs={{1,0},{2,1},{3,2},{4,3},{5,4},{6,5},{7,6},{8,7},{9,8},{10,9},{11,1... | collective-permute-start | bytes 98312 | tf_op jit(solution)/shard_map/ppermute | solution.py:17
  10.9 14.0 %collective-permute-start.2 = (f32[16,2,1,256]{3,2,1,0:T(1,128)S(1)}, f32[16,2,1,256]{3,2,1,0:T(1,128)S(1)}, u32[]{:S(2)}, u32[]{:S(2)}) collective-permute-start(f32[16,2,1,256]{3,2,1,0:T(1,128)S(1)} %get-tuple-element.44), channel_id=1, source_target_pairs={{0,1},{1,2},{2,3},{3,4},{4,5},{5,6},{6,7},{7,8},{8,9},{9,10},{10,1... | collective-permute-start | bytes 98312 | tf_op jit(solution)/shard_map/ppermute | solution.py:14
  15.6 165.5 %collective-permute-start.9 = (f32[16,2,1,256]{3,2,1,0:T(1,128)S(1)}, f32[16,2,1,256]{3,2,1,0:T(1,128)S(1)}, u32[]{:S(2)}, u32[]{:S(2)}) collective-permute-start(f32[16,2,1,256]{3,2,1,0:T(1,128)S(1)} %get-tuple-element.35), channel_id=1, source_target_pairs={{1,0},{2,1},{3,2},{4,3},{5,4},{6,5},{7,6},{8,7},{9,8},{10,9},{11,1... | collective-permute-start | bytes 98312 | tf_op jit(solution)/shard_map/ppermute | solution.py:17
  17.6 0.7 copy-start.2
  17.6 1.0 copy-start.1
  18.7 0.7 copy-start.6
  19.4 0.7 copy-start.3
  20.0 0.7 copy-start.7
  20.8 160.3 %collective-permute-start.8 = (f32[16,2,1,256]{3,2,1,0:T(1,128)S(1)}, f32[16,2,1,256]{3,2,1,0:T(1,128)S(1)}, u32[]{:S(2)}, u32[]{:S(2)}) collective-permute-start(f32[16,2,1,256]{3,2,1,0:T(1,128)S(1)} %get-tuple-element.34), channel_id=1, source_target_pairs={{0,1},{1,2},{2,3},{3,4},{4,5},{5,6},{6,7},{7,8},{8,9},{9,10},{10,1... | collective-permute-start | bytes 98312 | tf_op jit(solution)/shard_map/ppermute | solution.py:14
  25.1 5.7 %collective-permute-start.5 = (f32[16,2,1,256]{3,2,1,0:T(1,128)S(1)}, f32[16,2,1,256]{3,2,1,0:T(1,128)S(1)}, u32[]{:S(2)}, u32[]{:S(2)}) collective-permute-start(f32[16,2,1,256]{3,2,1,0:T(1,128)S(1)} %get-tuple-element.41), channel_id=1, source_target_pairs={{1,0},{2,1},{3,2},{4,3},{5,4},{6,5},{7,6},{8,7},{9,8},{10,9},{11,1... | collective-permute-start | bytes 98312 | tf_op jit(solution)/shard_map/ppermute | solution.py:17
  27.1 4.7 %collective-permute-start.4 = (f32[16,2,1,256]{3,2,1,0:T(1,128)S(1)}, f32[16,2,1,256]{3,2,1,0:T(1,128)S(1)}, u32[]{:S(2)}, u32[]{:S(2)}) collective-permute-start(f32[16,2,1,256]{3,2,1,0:T(1,128)S(1)} %get-tuple-element.40), channel_id=1, source_target_pairs={{0,1},{1,2},{2,3},{3,4},{4,5},{5,6},{6,7},{7,8},{8,9},{9,10},{10,1... | collective-permute-start | bytes 98312 | tf_op jit(solution)/shard_map/ppermute | solution.py:14
  122.7 5.7 %collective-permute-start.7 = (f32[16,2,1,256]{3,2,1,0:T(1,128)S(1)}, f32[16,2,1,256]{3,2,1,0:T(1,128)S(1)}, u32[]{:S(2)}, u32[]{:S(2)}) collective-permute-start(f32[16,2,1,256]{3,2,1,0:T(1,128)S(1)} %get-tuple-element.37), channel_id=1, source_target_pairs={{1,0},{2,1},{3,2},{4,3},{5,4},{6,5},{7,6},{8,7},{9,8},{10,9},{11,1... | collective-permute-start | bytes 98312 | tf_op jit(solution)/shard_map/ppermute | solution.py:17
  125.2 4.1 %collective-permute-start.6 = (f32[16,2,1,256]{3,2,1,0:T(1,128)S(1)}, f32[16,2,1,256]{3,2,1,0:T(1,128)S(1)}, u32[]{:S(2)}, u32[]{:S(2)}) collective-permute-start(f32[16,2,1,256]{3,2,1,0:T(1,128)S(1)} %get-tuple-element.36), channel_id=1, source_target_pairs={{0,1},{1,2},{2,3},{3,4},{4,5},{5,6},{6,7},{7,8},{8,9},{9,10},{10,1... | collective-permute-start | bytes 98312 | tf_op jit(solution)/shard_map/ppermute | solution.py:14
  158.4 0.7 copy-start.4
  179.4 0.7 copy-start.5
  181.5 7.7 %collective-permute-start.11 = (f32[16,2,1,256]{3,2,1,0:T(1,128)S(1)}, f32[16,2,1,256]{3,2,1,0:T(1,128)S(1)}, u32[]{:S(2)}, u32[]{:S(2)}) collective-permute-start(f32[16,2,1,256]{3,2,1,0:T(1,128)S(1)} %get-tuple-element.29), channel_id=1, source_target_pairs={{1,0},{2,1},{3,2},{4,3},{5,4},{6,5},{7,6},{8,7},{9,8},{10,9},{11,1... | collective-permute-start | bytes 98312 | tf_op jit(solution)/shard_map/ppermute | solution.py:17
  183.6 5.6 %collective-permute-start.10 = (f32[16,2,1,256]{3,2,1,0:T(1,128)S(1)}, f32[16,2,1,256]{3,2,1,0:T(1,128)S(1)}, u32[]{:S(2)}, u32[]{:S(2)}) collective-permute-start(f32[16,2,1,256]{3,2,1,0:T(1,128)S(1)} %get-tuple-element.28), channel_id=1, source_target_pairs={{0,1},{1,2},{2,3},{3,4},{4,5},{5,6},{6,7},{7,8},{8,9},{9,10},{10,1... | collective-permute-start | bytes 98312 | tf_op jit(solution)/shard_map/ppermute | solution.py:14
  187.2 130.6 %collective-permute-start.15 = (f32[16,2,1,256]{3,2,1,0:T(1,128)S(1)}, f32[16,2,1,256]{3,2,1,0:T(1,128)S(1)}, u32[]{:S(2)}, u32[]{:S(2)}) collective-permute-start(f32[16,2,1,256]{3,2,1,0:T(1,128)S(1)} %slice.268), channel_id=1, source_target_pairs={{1,0},{2,1},{3,2},{4,3},{5,4},{6,5},{7,6},{8,7},{9,8},{10,9},{11,1... | collective-permute-start | bytes 98312 | tf_op jit(solution)/shard_map/ppermute | solution.py:25
  277.9 5.7 %collective-permute-start.13 = (f32[16,2,1,256]{3,2,1,0:T(1,128)S(1)}, f32[16,2,1,256]{3,2,1,0:T(1,128)S(1)}, u32[]{:S(2)}, u32[]{:S(2)}) collective-permute-start(f32[16,2,1,256]{3,2,1,0:T(1,128)S(1)} %get-tuple-element.25), channel_id=1, source_target_pairs={{1,0},{2,1},{3,2},{4,3},{5,4},{6,5},{7,6},{8,7},{9,8},{10,9},{11,1... | collective-permute-start | bytes 98312 | tf_op jit(solution)/shard_map/ppermute | solution.py:17
  280.5 4.1 %collective-permute-start.12 = (f32[16,2,1,256]{3,2,1,0:T(1,128)S(1)}, f32[16,2,1,256]{3,2,1,0:T(1,128)S(1)}, u32[]{:S(2)}, u32[]{:S(2)}) collective-permute-start(f32[16,2,1,256]{3,2,1,0:T(1,128)S(1)} %get-tuple-element.24), channel_id=1, source_target_pairs={{0,1},{1,2},{2,3},{3,4},{4,5},{5,6},{6,7},{7,8},{8,9},{9,10},{10,1... | collective-permute-start | bytes 98312 | tf_op jit(solution)/shard_map/ppermute | solution.py:14
  313.6 5.2 %collective-permute-start.14 = (f32[16,2,1,256]{3,2,1,0:T(1,128)S(1)}, f32[16,2,1,256]{3,2,1,0:T(1,128)S(1)}, u32[]{:S(2)}, u32[]{:S(2)}) collective-permute-start(f32[16,2,1,256]{3,2,1,0:T(1,128)S(1)} %slice.266), channel_id=1, source_target_pairs={{1,0},{2,1},{3,2},{4,3},{5,4},{6,5},{7,6},{8,7},{9,8},{10,9},{11,1... | collective-permute-start | bytes 98312 | tf_op jit(solution)/shard_map/ppermute | solution.py:25
where the time goes:
time: 320 us
  blocking collectives  254 us (79%)
  starting transfers between devices  45.6 us (14%)
  local copies, waits for them, and re-layouts  9.47 us (3%)
  other arithmetic  4.88 us (2%)
  waiting for transfers between devices  3.57 us (1%)
    psum x4, blocking collectives, squares(): return lax.psum(local_sum(residual, residual), 'col')  178 us
    psum x2, blocking collectives, conjugate(): step_size = norm_now / lax.psum(local_sum(direction, applied), 'col')  57 us
    ppermute x7, starting transfers between devices, padded_2(): lax.ppermute(lax.slice_in_dim(block, block.shape[dim] - width, None, axis...  25.1 us
    all_gather x1, blocking collectives, on_device(): potentials = lax.all_gather(own_potentials, 'col', axis=1, tiled=True)  19 us
    ppermute x7, starting transfers between devices, padded_2(): lax.ppermute(lax.slice_in_dim(block, 0, width, axis=dim), axis, backward)  14.8 us
  transfers between devices with their start and end apart: 16, of which 4 were waited for; matrix products, arithmetic and copies ran while one was open for 3% of the time, Pallas kernels for 0%

commit v1 on v0

--- a/solution.py
+++ b/solution.py
@@ -71,7 +71,12 @@
     for iteration in range(ITERS):
         if iteration > 0:
             applied = operate(direction)
-        step_size = norm_now / lax.psum(local_sum(direction, applied), "col")
+
+        def form_scenes_here(mat):
+            known = jnp.sum(lax.all_gather(mat, axis_name="col"), 0)
+            return known
+
+        step_size = norm_now / form_scenes_here(local_sum(direction, applied))
         solution = solution + expand(step_size) * direction
         if iteration + 1 < ITERS:
             residual = residual - expand(step_size) * applied

time: 320 us -> 282 us (0.88)
  blocking collectives: 254 us -> 213 us
    all_gather x0 -> x4, blocking collectives: none -> 78.4 us  [form_scenes_here(): known = jnp.sum(lax.all_gather(mat, axis_name='col'), 0)]
    psum x4, blocking collectives: 178 us -> 117 us  [squares(): return lax.psum(local_sum(residual, residual), 'col')]
    psum x2 -> x0, blocking collectives: 57 us -> none  [conjugate(): step_size = norm_now / lax.psum(local_sum(direction, applied), 'col')]
    ppermute x7, starting transfers between devices: 14.8 us -> 18.8 us  [padded_2(): lax.ppermute(lax.slice_in_dim(block, 0, width, axis=dim), axis, backward)]
  transfers between devices with their start and end apart: 16 -> 16, of which waited for: 4 -> 4; matrix products, arithmetic and copies ran while one was open for 3% -> 4% of each run, Pallas kernels for 0% -> 0%
where the time goes in v1:
time: 282 us
  blocking collectives  213 us (76%)
  starting transfers between devices  45.6 us (16%)
  local copies, waits for them, and re-layouts  10.1 us (4%)
  waiting for transfers between devices  5.74 us (2%)
  other arithmetic  5.02 us (2%)
    psum x4, blocking collectives, squares(): return lax.psum(local_sum(residual, residual), 'col')  117 us
    all_gather x4, blocking collectives, form_scenes_here(): known = jnp.sum(lax.all_gather(mat, axis_name='col'), 0)  78.4 us
    ppermute x7, starting transfers between devices, padded_2(): lax.ppermute(lax.slice_in_dim(block, block.shape[dim] - width, None, axis...  22.8 us
    ppermute x7, starting transfers between devices, padded_2(): lax.ppermute(lax.slice_in_dim(block, 0, width, axis=dim), axis, backward)  18.8 us
    all_gather x1, blocking collectives, on_device(): potentials = lax.all_gather(own_potentials, 'col', axis=1, tiled=True)  17.5 us
  transfers between devices with their start and end apart: 16, of which 4 were waited for; matrix products, arithmetic and copies ran while one was open for 4% of the time, Pallas kernels for 0%

profile of v1, /device:TPU:1, one launch (start us, length us, event | category | flops | bytes accessed | tf_op | source)
XLA Modules:
  0.0 281.7 jit_solution(9320839059144562574)
XLA Ops:
  1.4 1.9 collective-permute-start.1
  3.3 4.5 %collective-permute-start = (f32[2,256]{1,0:T(2,128)S(1)}, f32[2,256]{1,0:T(2,128)S(1)}, u32[]{:S(2)}, u32[]{:S(2)}) collective-permute-start(f32[2,256]{1,0:T(2,128)S(1)} %get-tuple-element.61), channel_id=1, source_target_pairs={{0,1},{1,2},{2,3},{3,4},{4,5},{5,6},{6,7},{7,8},{8,9},{9,10},{10,1... | collective-permute-start | bytes 6152 | tf_op jit(solution)/shard_map/ppermute | solution.py:14
  7.9 1.1 fusion.93
  9.0 1.9 collective-permute-start.3
  10.9 3.6 %collective-permute-start.2 = (f32[16,2,1,256]{3,2,1,0:T(1,128)S(1)}, f32[16,2,1,256]{3,2,1,0:T(1,128)S(1)}, u32[]{:S(2)}, u32[]{:S(2)}) collective-permute-start(f32[16,2,1,256]{3,2,1,0:T(1,128)S(1)} %get-tuple-element.44), channel_id=1, source_target_pairs={{0,1},{1,2},{2,3},{3,4},{4,5},{5,6},{6,7},{7,8},{8,9},{9,10},{10,1... | collective-permute-start | bytes 98312 | tf_op jit(solution)/shard_map/ppermute | solution.py:14
  14.5 1.1 fusion.88
  15.6 1.9 collective-permute-start.9
  20.8 3.6 %collective-permute-start.8 = (f32[16,2,1,256]{3,2,1,0:T(1,128)S(1)}, f32[16,2,1,256]{3,2,1,0:T(1,128)S(1)}, u32[]{:S(2)}, u32[]{:S(2)}) collective-permute-start(f32[16,2,1,256]{3,2,1,0:T(1,128)S(1)} %get-tuple-element.34), channel_id=1, source_target_pairs={{0,1},{1,2},{2,3},{3,4},{4,5},{5,6},{6,7},{7,8},{8,9},{9,10},{10,1... | collective-permute-start | bytes 98312 | tf_op jit(solution)/shard_map/ppermute | solution.py:14
  25.1 1.9 collective-permute-start.5
  27.1 3.6 %collective-permute-start.4 = (f32[16,2,1,256]{3,2,1,0:T(1,128)S(1)}, f32[16,2,1,256]{3,2,1,0:T(1,128)S(1)}, u32[]{:S(2)}, u32[]{:S(2)}) collective-permute-start(f32[16,2,1,256]{3,2,1,0:T(1,128)S(1)} %get-tuple-element.40), channel_id=1, source_target_pairs={{0,1},{1,2},{2,3},{3,4},{4,5},{5,6},{6,7},{7,8},{8,9},{9,10},{10,1... | collective-permute-start | bytes 98312 | tf_op jit(solution)/shard_map/ppermute | solution.py:14
  30.9 0.9 collective-permute-done.4
  32.1 30.8 %psum.28 = f32[16,2]{1,0:T(8,128)S(1)} all-reduce(f32[16,2]{1,0:T(8,128)S(1)} %get-tuple-element.17), channel_id=1, replica_groups=mesh['lines'=2,'col'=16] {'col'}, use_global_device_ids=true, to_apply=%region_1.2 | all-reduce | flops 32 | bytes 256 | tf_op jit(solution)/shard_map/psum | solution.py:58
  63.0 19.4 %all-gather.4 = f32[16,16,2]{1,2,0:T(2,128)S(1)} all-gather(f32[1,16,2]{1,2,0:T(2,128)S(1)} %bitcast.31), channel_id=2, replica_groups=mesh['lines'=2,'col'=16] {'col'}, dimensions={0}, use_global_device_ids=true | all-gather | bytes 2176 | tf_op jit(solution)/shard_map/all_gather | solution.py:76
  82.8 29.5 %psum.29 = f32[16,2]{1,0:T(8,128)S(1)} all-reduce(f32[16,2]{1,0:T(8,128)S(1)} %multiply_reduce_fusion.3), channel_id=1, replica_groups=mesh['lines'=2,'col'=16] {'col'}, use_global_device_ids=true, to_apply=%region_5.6 | all-reduce | flops 32 | bytes 256 | tf_op jit(solution)/shard_map/psum | solution.py:58
  112.5 4.5 %collective-permute-start.7 = (f32[16,2,1,256]{3,2,1,0:T(1,128)S(1)}, f32[16,2,1,256]{3,2,1,0:T(1,128)S(1)}, u32[]{:S(2)}, u32[]{:S(2)}) collective-permute-start(f32[16,2,1,256]{3,2,1,0:T(1,128)S(1)} %get-tuple-element.37), channel_id=1, source_target_pairs={{1,0},{2,1},{3,2},{4,3},{5,4},{6,5},{7,6},{8,7},{9,8},{10,9},{11,1... | collective-permute-start | bytes 98312 | tf_op jit(solution)/shard_map/ppermute | solution.py:17
  117.0 1.9 collective-permute-start.6
  119.1 1.0 collective-permute-done.6
  120.5 19.5 %all-gather.5 = f32[16,16,2]{1,2,0:T(2,128)S(1)} all-gather(f32[1,16,2]{1,2,0:T(2,128)S(1)} %bitcast.32), channel_id=3, replica_groups=mesh['lines'=2,'col'=16] {'col'}, dimensions={0}, use_global_device_ids=true | all-gather | bytes 2176 | tf_op jit(solution)/shard_map/all_gather | solution.py:76
  141.4 17.5 %all-gather.6 = f32[16,2,2]{2,1,0:T(2,128)S(1)} all-gather(f32[1,2,2]{2,1,0:T(2,128)S(1)} %convolution_bitcast_fusion), channel_id=1, replica_groups=mesh['lines'=2,'col'=16] {'col'}, dimensions={0}, use_global_device_ids=true | all-gather | bytes 272 | tf_op jit(solution)/shard_map/all_gather | solution.py:117
  158.9 0.9 gather_fusion
  161.9 2.1 collective-permute-start.11
  164.0 3.5 %collective-permute-start.10 = (f32[16,2,1,256]{3,2,1,0:T(1,128)S(1)}, f32[16,2,1,256]{3,2,1,0:T(1,128)S(1)}, u32[]{:S(2)}, u32[]{:S(2)}) collective-permute-start(f32[16,2,1,256]{3,2,1,0:T(1,128)S(1)} %get-tuple-element.28), channel_id=1, source_target_pairs={{0,1},{1,2},{2,3},{3,4},{4,5},{5,6},{6,7},{7,8},{8,9},{9,10},{10,1... | collective-permute-start | bytes 98312 | tf_op jit(solution)/shard_map/ppermute | solution.py:14
  167.7 1.9 collective-permute-start.15
  170.0 27.6 %psum.30 = f32[16,2]{1,0:T(8,128)S(1)} all-reduce(f32[16,2]{1,0:T(8,128)S(1)} %get-tuple-element.15), channel_id=1, replica_groups=mesh['lines'=2,'col'=16] {'col'}, use_global_device_ids=true, to_apply=%region_9.10 | all-reduce | flops 32 | bytes 256 | tf_op jit(solution)/shard_map/psum | solution.py:58
  197.7 20.1 %all-gather.7 = f32[16,16,2]{1,2,0:T(2,128)S(1)} all-gather(f32[1,16,2]{1,2,0:T(2,128)S(1)} %bitcast.33), channel_id=4, replica_groups=mesh['lines'=2,'col'=16] {'col'}, dimensions={0}, use_global_device_ids=true | all-gather | bytes 2176 | tf_op jit(solution)/shard_map/all_gather | solution.py:76
  218.1 29.5 %psum.31 = f32[16,2]{1,0:T(8,128)S(1)} all-reduce(f32[16,2]{1,0:T(8,128)S(1)} %multiply_reduce_fusion), channel_id=1, replica_groups=mesh['lines'=2,'col'=16] {'col'}, use_global_device_ids=true, to_apply=%region_13.14 | all-reduce | flops 32 | bytes 256 | tf_op jit(solution)/shard_map/psum | solution.py:58
  247.8 4.5 %collective-permute-start.13 = (f32[16,2,1,256]{3,2,1,0:T(1,128)S(1)}, f32[16,2,1,256]{3,2,1,0:T(1,128)S(1)}, u32[]{:S(2)}, u32[]{:S(2)}) collective-permute-start(f32[16,2,1,256]{3,2,1,0:T(1,128)S(1)} %get-tuple-element.25), channel_id=1, source_target_pairs={{1,0},{2,1},{3,2},{4,3},{5,4},{6,5},{7,6},{8,7},{9,8},{10,9},{11,1... | collective-permute-start | bytes 98312 | tf_op jit(solution)/shard_map/ppermute | solution.py:17
  252.4 1.9 collective-permute-start.12
  254.4 1.0 collective-permute-done.12
  255.9 19.5 %all-gather.8 = f32[16,16,2]{1,2,0:T(2,128)S(1)} all-gather(f32[1,16,2]{1,2,0:T(2,128)S(1)} %bitcast.34), channel_id=5, replica_groups=mesh['lines'=2,'col'=16] {'col'}, dimensions={0}, use_global_device_ids=true | all-gather | bytes 2176 | tf_op jit(solution)/shard_map/all_gather | solution.py:76
  275.7 2.1 collective-permute-start.14
  278.1 2.8 collective-permute-done.14
  (100 shorter events, 12.9 us)
Async XLA Ops:
  0.6 16.9 %copy-start = (f32[16,2,8,256]{3,2,1,0:T(8,128)S(1)}, f32[16,2,8,256]{3,2,1,0:T(8,128)}, u32[]{:S(2)}) copy-start(f32[16,2,8,256]{3,2,1,0:T(8,128)} %param.8) | copy-start | bytes 786436
  1.4 19.4 %collective-permute-start.1 = (f32[2,256]{1,0:T(2,128)S(1)}, f32[2,256]{1,0:T(2,128)S(1)}, u32[]{:S(2)}, u32[]{:S(2)}) collective-permute-start(f32[2,256]{1,0:T(2,128)S(1)} %get-tuple-element.62), channel_id=1, source_target_pairs={{1,0},{2,1},{3,2},{4,3},{5,4},{6,5},{7,6},{8,7},{9,8},{10,9},{11,1... | collective-permute-start | bytes 6152 | tf_op jit(solution)/shard_map/ppermute | solution.py:17
  3.3 21.1 %collective-permute-start = (f32[2,256]{1,0:T(2,128)S(1)}, f32[2,256]{1,0:T(2,128)S(1)}, u32[]{:S(2)}, u32[]{:S(2)}) collective-permute-start(f32[2,256]{1,0:T(2,128)S(1)} %get-tuple-element.61), channel_id=1, source_target_pairs={{0,1},{1,2},{2,3},{3,4},{4,5},{5,6},{6,7},{7,8},{8,9},{9,10},{10,1... | collective-permute-start | bytes 6152 | tf_op jit(solution)/shard_map/ppermute | solution.py:14
  9.0 15.9 %collective-permute-start.3 = (f32[16,2,1,256]{3,2,1,0:T(1,128)S(1)}, f32[16,2,1,256]{3,2,1,0:T(1,128)S(1)}, u32[]{:S(2)}, u32[]{:S(2)}) collective-permute-start(f32[16,2,1,256]{3,2,1,0:T(1,128)S(1)} %get-tuple-element.45), channel_id=1, source_target_pairs={{1,0},{2,1},{3,2},{4,3},{5,4},{6,5},{7,6},{8,7},{9,8},{10,9},{11,1... | collective-permute-start | bytes 98312 | tf_op jit(solution)/shard_map/ppermute | solution.py:17
  10.9 14.0 %collective-permute-start.2 = (f32[16,2,1,256]{3,2,1,0:T(1,128)S(1)}, f32[16,2,1,256]{3,2,1,0:T(1,128)S(1)}, u32[]{:S(2)}, u32[]{:S(2)}) collective-permute-start(f32[16,2,1,256]{3,2,1,0:T(1,128)S(1)} %get-tuple-element.44), channel_id=1, source_target_pairs={{0,1},{1,2},{2,3},{3,4},{4,5},{5,6},{6,7},{7,8},{8,9},{9,10},{10,1... | collective-permute-start | bytes 98312 | tf_op jit(solution)/shard_map/ppermute | solution.py:14
  15.6 145.9 %collective-permute-start.9 = (f32[16,2,1,256]{3,2,1,0:T(1,128)S(1)}, f32[16,2,1,256]{3,2,1,0:T(1,128)S(1)}, u32[]{:S(2)}, u32[]{:S(2)}) collective-permute-start(f32[16,2,1,256]{3,2,1,0:T(1,128)S(1)} %get-tuple-element.35), channel_id=1, source_target_pairs={{1,0},{2,1},{3,2},{4,3},{5,4},{6,5},{7,6},{8,7},{9,8},{10,9},{11,1... | collective-permute-start | bytes 98312 | tf_op jit(solution)/shard_map/ppermute | solution.py:17
  17.6 0.7 copy-start.2
  17.6 1.0 copy-start.1
  18.7 0.7 copy-start.6
  19.4 0.7 copy-start.3
  20.0 0.7 copy-start.7
  20.8 140.8 %collective-permute-start.8 = (f32[16,2,1,256]{3,2,1,0:T(1,128)S(1)}, f32[16,2,1,256]{3,2,1,0:T(1,128)S(1)}, u32[]{:S(2)}, u32[]{:S(2)}) collective-permute-start(f32[16,2,1,256]{3,2,1,0:T(1,128)S(1)} %get-tuple-element.34), channel_id=1, source_target_pairs={{0,1},{1,2},{2,3},{3,4},{4,5},{5,6},{6,7},{7,8},{8,9},{9,10},{10,1... | collective-permute-start | bytes 98312 | tf_op jit(solution)/shard_map/ppermute | solution.py:14
  25.1 5.7 %collective-permute-start.5 = (f32[16,2,1,256]{3,2,1,0:T(1,128)S(1)}, f32[16,2,1,256]{3,2,1,0:T(1,128)S(1)}, u32[]{:S(2)}, u32[]{:S(2)}) collective-permute-start(f32[16,2,1,256]{3,2,1,0:T(1,128)S(1)} %get-tuple-element.41), channel_id=1, source_target_pairs={{1,0},{2,1},{3,2},{4,3},{5,4},{6,5},{7,6},{8,7},{9,8},{10,9},{11,1... | collective-permute-start | bytes 98312 | tf_op jit(solution)/shard_map/ppermute | solution.py:17
  27.1 4.7 %collective-permute-start.4 = (f32[16,2,1,256]{3,2,1,0:T(1,128)S(1)}, f32[16,2,1,256]{3,2,1,0:T(1,128)S(1)}, u32[]{:S(2)}, u32[]{:S(2)}) collective-permute-start(f32[16,2,1,256]{3,2,1,0:T(1,128)S(1)} %get-tuple-element.40), channel_id=1, source_target_pairs={{0,1},{1,2},{2,3},{3,4},{4,5},{5,6},{6,7},{7,8},{8,9},{9,10},{10,1... | collective-permute-start | bytes 98312 | tf_op jit(solution)/shard_map/ppermute | solution.py:14
  112.5 6.6 %collective-permute-start.7 = (f32[16,2,1,256]{3,2,1,0:T(1,128)S(1)}, f32[16,2,1,256]{3,2,1,0:T(1,128)S(1)}, u32[]{:S(2)}, u32[]{:S(2)}) collective-permute-start(f32[16,2,1,256]{3,2,1,0:T(1,128)S(1)} %get-tuple-element.37), channel_id=1, source_target_pairs={{1,0},{2,1},{3,2},{4,3},{5,4},{6,5},{7,6},{8,7},{9,8},{10,9},{11,1... | collective-permute-start | bytes 98312 | tf_op jit(solution)/shard_map/ppermute | solution.py:17
  117.0 3.1 %collective-permute-start.6 = (f32[16,2,1,256]{3,2,1,0:T(1,128)S(1)}, f32[16,2,1,256]{3,2,1,0:T(1,128)S(1)}, u32[]{:S(2)}, u32[]{:S(2)}) collective-permute-start(f32[16,2,1,256]{3,2,1,0:T(1,128)S(1)} %get-tuple-element.36), channel_id=1, source_target_pairs={{0,1},{1,2},{2,3},{3,4},{4,5},{5,6},{6,7},{7,8},{8,9},{9,10},{10,1... | collective-permute-start | bytes 98312 | tf_op jit(solution)/shard_map/ppermute | solution.py:14
  140.3 0.7 copy-start.4
  159.8 0.7 copy-start.5
  161.9 7.7 %collective-permute-start.11 = (f32[16,2,1,256]{3,2,1,0:T(1,128)S(1)}, f32[16,2,1,256]{3,2,1,0:T(1,128)S(1)}, u32[]{:S(2)}, u32[]{:S(2)}) collective-permute-start(f32[16,2,1,256]{3,2,1,0:T(1,128)S(1)} %get-tuple-element.29), channel_id=1, source_target_pairs={{1,0},{2,1},{3,2},{4,3},{5,4},{6,5},{7,6},{8,7},{9,8},{10,9},{11,1... | collective-permute-start | bytes 98312 | tf_op jit(solution)/shard_map/ppermute | solution.py:17
  164.0 5.6 %collective-permute-start.10 = (f32[16,2,1,256]{3,2,1,0:T(1,128)S(1)}, f32[16,2,1,256]{3,2,1,0:T(1,128)S(1)}, u32[]{:S(2)}, u32[]{:S(2)}) collective-permute-start(f32[16,2,1,256]{3,2,1,0:T(1,128)S(1)} %get-tuple-element.28), channel_id=1, source_target_pairs={{0,1},{1,2},{2,3},{3,4},{4,5},{5,6},{6,7},{7,8},{8,9},{9,10},{10,1... | collective-permute-start | bytes 98312 | tf_op jit(solution)/shard_map/ppermute | solution.py:14
  167.7 110.4 %collective-permute-start.15 = (f32[16,2,1,256]{3,2,1,0:T(1,128)S(1)}, f32[16,2,1,256]{3,2,1,0:T(1,128)S(1)}, u32[]{:S(2)}, u32[]{:S(2)}) collective-permute-start(f32[16,2,1,256]{3,2,1,0:T(1,128)S(1)} %slice.268), channel_id=1, source_target_pairs={{1,0},{2,1},{3,2},{4,3},{5,4},{6,5},{7,6},{8,7},{9,8},{10,9},{11,1... | collective-permute-start | bytes 98312 | tf_op jit(solution)/shard_map/ppermute | solution.py:25
  247.8 6.6 %collective-permute-start.13 = (f32[16,2,1,256]{3,2,1,0:T(1,128)S(1)}, f32[16,2,1,256]{3,2,1,0:T(1,128)S(1)}, u32[]{:S(2)}, u32[]{:S(2)}) collective-permute-start(f32[16,2,1,256]{3,2,1,0:T(1,128)S(1)} %get-tuple-element.25), channel_id=1, source_target_pairs={{1,0},{2,1},{3,2},{4,3},{5,4},{6,5},{7,6},{8,7},{9,8},{10,9},{11,1... | collective-permute-start | bytes 98312 | tf_op jit(solution)/shard_map/ppermute | solution.py:17
  252.4 3.1 %collective-permute-start.12 = (f32[16,2,1,256]{3,2,1,0:T(1,128)S(1)}, f32[16,2,1,256]{3,2,1,0:T(1,128)S(1)}, u32[]{:S(2)}, u32[]{:S(2)}) collective-permute-start(f32[16,2,1,256]{3,2,1,0:T(1,128)S(1)} %get-tuple-element.24), channel_id=1, source_target_pairs={{0,1},{1,2},{2,3},{3,4},{4,5},{5,6},{6,7},{7,8},{8,9},{9,10},{10,1... | collective-permute-start | bytes 98312 | tf_op jit(solution)/shard_map/ppermute | solution.py:14
  275.7 5.2 %collective-permute-start.14 = (f32[16,2,1,256]{3,2,1,0:T(1,128)S(1)}, f32[16,2,1,256]{3,2,1,0:T(1,128)S(1)}, u32[]{:S(2)}, u32[]{:S(2)}) collective-permute-start(f32[16,2,1,256]{3,2,1,0:T(1,128)S(1)} %slice.266), channel_id=1, source_target_pairs={{1,0},{2,1},{3,2},{4,3},{5,4},{6,5},{7,6},{8,7},{9,8},{10,9},{11,1... | collective-permute-start | bytes 98312 | tf_op jit(solution)/shard_map/ppermute | solution.py:25
